TPU v7x, 32 devices: a whole 2x2x4 slice. The times are simulated.
32 devices in a mesh: dp: 8 (over z, y), mp: 4 (over x, core).
Axes of the slice: x: 2, y: 2, z: 4, core: 2. Of those that a mesh axis runs over, the one named last changes fastest.
Arguments:
- gradients: bfloat16 [8, 4, 192, 16384], P('dp', 'mp'), may hold values from -3000 to 3000
- owner_list: int32 [192], replicated, may hold values from 0 to 7, as said below
- master_weights: float32 [4, 288, 16384], P('mp', 'dp'), may hold values from -6 to 6
- first_moment: float32 [4, 288, 16384], P('mp', 'dp'), may hold values from -6 to 6
- second_moment: float32 [4, 288, 16384], P('mp', 'dp'), may hold values from 0.05 to 2
- average_weights: float32 [4, 288, 16384], P('mp', 'dp'), may hold values from -6 to 6
Outputs:
- new_params: bfloat16 [4, 192, 16384], P('mp')
- new_master: float32 [4, 288, 16384], P('mp', 'dp')
- new_first: float32 [4, 288, 16384], P('mp', 'dp')
- new_second: float32 [4, 288, 16384], P('mp', 'dp')
- average_rows: float32 [4, 192, 16384], P('mp', 'dp')
Inputs may be any that keep to these rules, and one draw needn't show every extreme that they name: `owner_list`: each data rank owns at most 36 segments, and some rank owns exactly 36.
All inputs are finite; a program needn't handle non-finite values.
Results may differ from a plain program's by a relative error of at most 0.015.
Values may be sent and summed in bfloat16 or wider, within the bound.
No kernel may reach another device: no remote copies, remote signals or barrier semaphores. Data moves between devices by JAX's collectives and lax.ppermute only.
A program may use at most 128 MiB of HBM per device.

v0:
```python
import math
import jax
import jax.numpy as jnp
from jax import lax
from jax.sharding import PartitionSpec as P


def slot_matrix(owner_list, ranks, cap):
    count = owner_list.shape[0]
    position = jnp.arange(count, dtype=jnp.int32)
    same_owner = (owner_list[:, None] == owner_list[None, :]) & (
        position[None, :] < position[:, None]
    )
    slot_index = owner_list * cap + jnp.sum(same_owner.astype(jnp.int32), axis=1)
    rows = jnp.arange(ranks * cap, dtype=jnp.int32)
    return (rows[:, None] == slot_index[None, :]).astype(jnp.float32)


def on_device(gradients, owner_list, master_weights, first_moment, second_moment, average_weights):
    highest = lax.Precision.HIGHEST
    local_grad = gradients[0, 0]
    nseg, seg = local_grad.shape
    cap = master_weights.shape[1]
    ranks = lax.axis_size("dp")
    blocks = lax.axis_size("mp")
    per_rank = nseg // ranks
    my_rank = lax.axis_index("dp")
    placing = slot_matrix(owner_list, ranks, cap)
    my_slots = lax.dynamic_slice_in_dim(placing, my_rank * cap, cap, 0)
    in_use = jnp.sum(my_slots, axis=1)[:, None]
    summed = lax.psum(local_grad.astype(jnp.float32).astype(jnp.bfloat16), "dp").astype(jnp.float32)
    total_sq = lax.psum(jnp.sum(summed * summed), "mp")
    owned_grad = jnp.dot(my_slots, summed, precision=highest)
    clip_factor = jnp.minimum(1.0, math.sqrt(blocks * nseg * seg) / (jnp.sqrt(total_sq) + 1e-06))
    owned_grad = clip_factor * owned_grad
    new_first = in_use * (0.9 * first_moment[0] + 0.1 * owned_grad)
    new_second = in_use * (0.95 * second_moment[0] + 0.05 * owned_grad * owned_grad)
    first_hat = new_first / (1.0 - 0.9**20)
    second_hat = new_second / (1.0 - 0.95**20)
    old_master = master_weights[0]
    new_master = in_use * (
        old_master - 0.02 * (first_hat / (jnp.sqrt(second_hat) + 1e-08) + 0.1 * old_master)
    )
    averaged = 0.9 * average_weights[0] + 0.1 * new_master
    placing_rows = placing.T
    placing_half = placing_rows.astype(jnp.bfloat16)
    gathered = jnp.dot(
        placing_half,
        lax.all_gather(new_master.astype(jnp.bfloat16), "dp", axis=0, tiled=True),
        preferred_element_type=jnp.float32,
    )
    new_params = gathered.astype(jnp.bfloat16)
    spread_out = jnp.dot(my_slots.T, averaged, precision=highest).reshape(ranks, per_rank, seg)
    arrived = lax.all_to_all(spread_out, "dp", split_axis=0, concat_axis=0, tiled=True)
    average_rows = jnp.sum(arrived, axis=0)
    return (
        new_params[None],
        new_master[None],
        new_first[None],
        new_second[None],
        average_rows[None],
    )


def solution(mesh):
    return jax.shard_map(
        on_device,
        mesh=mesh,
        in_specs=(
            P("dp", "mp", None, None),
            P(),
            P("mp", "dp", None),
            P("mp", "dp", None),
            P("mp", "dp", None),
            P("mp", "dp", None),
        ),
        out_specs=(
            P("mp", None, None),
            P("mp", "dp", None),
            P("mp", "dp", None),
            P("mp", "dp", None),
            P("mp", "dp", None),
        ),
        check_vma=False,
    )
```

profile of v0, /device:TPU:0, one launch (start us, length us, event | category | flops | bytes accessed | tf_op | source)
XLA Modules:
  0.0 680.6 jit_solution(15627968808862761865)
XLA Ops:
  7.2 0.0 all-reduce.2.cloned.1.call-start
  7.2 0.0 copy-start.3
  7.2 0.7 all-reduce.2.cloned.1.call-update
  7.9 0.0 copy-done.3
  7.9 0.2 convert_reduce_fusion
  8.2 217.6 %all-reduce.2.cloned.1.call-done = bf16[192,16384]{1,0:T(8,128)(2,1)} async-done(((bf16[192,16384]{1,0:T(8,128)(2,1)}), bf16[192,16384]{1,0:T(8,128)(2,1)}) %all-reduce.2.cloned.1.call-update) | async-done | bytes 6291472 | tf_op jit(solution)/shard_map/psum | solution.py:31
  225.8 6.6 multiply_reduce_fusion
  232.4 0.1 convert_reduce_fusion.1
  232.5 7.7 %psum.15 = f32[]{:T(128)} all-reduce(f32[]{:T(128)} %multiply_reduce_fusion), channel_id=1, replica_groups=mesh['dp'=8,'mp'=4] {'mp'}, use_global_device_ids=true, to_apply=%region_4.0 | all-reduce | flops 1 | bytes 8 | tf_op jit(solution)/shard_map/psum | solution.py:32
  240.9 0.0 copy-start
  240.9 14.0 %convert_bitcast_fusion = (bf16[1,36,16384]{2,1,0:T(8,128)(2,1)}, f32[36,16384]{1,0:T(8,128)S(1)}, f32[1,36,16384]{2,1,0:T(8,128)}, f32[1,36,16384]{2,1,0:T(8,128)}) fusion(f32[1,36,16384]{2,0,1:T(1,128)} %param.10, f32[1,36,16384]{2,0,1:T(1,128)} %param.9, f32[1,36,16384]{2,0,1:T(1,128)} %param.8, f32[36]{0:T(128)S(1)} %convert_reduce_fusion.1, ...), kind=kOutput, calls=%fused_computation.20 | convolution fusion | flops 238288896 | bytes 21637640 | tf_op jit(solution)/shard_map/dot_general | solution.py:33
  254.9 0.0 copy-done
  254.9 8.4 %fusion.6 = f32[192,16384]{1,0:T(8,128)} fusion(f32[1,36,16384]{2,0,1:T(1,128)S(1)} %copy-done, f32[36,16384]{1,0:T(8,128)S(1)} %get-tuple-element.26, pred[288,192]{1,0:T(8,128)(4,1)S(1)} %iota_compare_fusion, s32[]{:T(128)S(6)} %select_n.3), kind=kOutput, calls=%fused_computation.13 | convolution fusion | flops 1360723968 | bytes 17573892 | tf_op jit(solution)/shard_map/dot_general | solution.py:53
  263.4 5.3 all-to-all-start
  268.7 0.3 all-gather.3.cloned.1.call-start
  269.0 0.5 all-gather.3.cloned.1.call-update
  269.5 0.0 copy-start.2
  269.5 3.8 copy.32
  273.3 0.0 copy-start.1
  273.3 0.0 copy-done.2
  273.3 3.8 copy.33
  277.2 0.0 copy-done.1
  277.2 3.8 copy.34
  281.0 362.5 %all-gather.3.cloned.1.call-done = bf16[8,36,16384]{2,1,0:T(8,128)(2,1)} async-done(((bf16[1,36,16384]{2,1,0:T(8,128)(2,1)}), bf16[8,36,16384]{2,1,0:T(8,128)(2,1)}) %all-gather.3.cloned.1.call-update) | async-done | bytes 9437200 | tf_op jit(solution)/shard_map/all_gather | solution.py:49
  643.5 8.5 %reshape.25 = bf16[288,16384]{1,0:T(8,128)(2,1)} reshape(bf16[8,36,16384]{2,1,0:T(8,128)(2,1)} %all-gather.3.cloned.1.call-done) | data formatting | bytes 18874368
  652.0 9.9 %fusion = bf16[1,192,16384]{2,1,0:T(8,128)(2,1)} fusion(bf16[288,16384]{1,0:T(8,128)(2,1)} %reshape.25, s32[192]{0:T(256)S(1)} %multiply_add_fusion), kind=kOutput, calls=%fused_computation.1 | convolution fusion | flops 1815250944 | bytes 15729408 | tf_op jit(solution)/shard_map/dot_general | solution.py:47
  661.8 5.4 all-to-all-done
  667.2 6.5 reduce_sum.39
  (2 shorter events, 0.1 us)
Async XLA Ops:
  7.2 218.6 %all-reduce.2.cloned.1.call-start = ((), (), s32[]{:S(2)}) async-start(), calls=%async_computation.1 | async-start | bytes 12582912 | tf_op jit(solution)/shard_map/psum | solution.py:31
  7.2 0.7 copy-start.3
  240.9 14.0 %copy-start = (f32[1,36,16384]{2,0,1:T(1,128)S(1)}, f32[1,36,16384]{2,0,1:T(1,128)}, u32[]{:S(2)}) copy-start(f32[1,36,16384]{2,0,1:T(1,128)} %param.11) | copy-start | bytes 7077892
  263.4 403.8 %all-to-all-start = ((f32[8,24,16384]{2,1,0:T(8,128)}), f32[8,24,16384]{2,1,0:T(8,128)}, u32[]{:S(2)}, u32[]{:S(2)}) async-start(f32[8,24,16384]{2,1,0:T(8,128)} %bitcast.45), calls=%async_computation | async-start | bytes 25165824 | tf_op jit(solution)/shard_map/all_to_all | solution.py:54
  268.7 374.8 %all-gather.3.cloned.1.call-start = ((), (), s32[]{:S(2)}) async-start(), calls=%async_computation.2 | async-start | bytes 11796480 | tf_op jit(solution)/shard_map/all_gather | solution.py:49
  269.5 3.8 copy-start.2
  273.3 3.8 copy-start.1
Sparse Core Ops, SparseCore 0:
  11.8 213.9 all-reduce.1
  272.6 370.8 all-gather.2
where the time goes:
time: 681 us
  waiting for transfers between devices  587 us (86%)
  matrix products  32.3 us (5%)
  local copies, waits for them, and re-layouts  20 us (3%)
  between operations  14.8 us (2%)
  other arithmetic  13.5 us (2%)
  blocking collectives  7.68 us (1%)
    all_gather x1, waiting for transfers between devices, on_device(): lax.all_gather(new_master.astype(jnp.bfloat16), 'dp', axis=0, tiled=True)  362 us
    psum x1, waiting for transfers between devices, on_device(): lax.psum(local_grad.astype(jnp.float32).astype(jnp.bfloat16), 'dp')  218 us
    unnamed x12, local copies, waits for them, and re-layouts  20 us
    dot_general x1, matrix products, on_device(): owned_grad = jnp.dot(my_slots, summed, precision=highest)  14 us
  transfers between devices with their start and end apart: 3, of which 3 were waited for; matrix products, arithmetic and copies ran while one was open for 4% of the time, Pallas kernels for 0%

commit v1 on v0

--- a/solution.py
+++ b/solution.py
@@ -28,7 +28,9 @@
     placing = slot_matrix(owner_list, ranks, cap)
     my_slots = lax.dynamic_slice_in_dim(placing, my_rank * cap, cap, 0)
     in_use = jnp.sum(my_slots, axis=1)[:, None]
-    summed = lax.psum(local_grad.astype(jnp.float32).astype(jnp.bfloat16), "dp").astype(jnp.float32)
+    summed = jnp.sum(
+        lax.all_gather(local_grad.astype(jnp.float32).astype(jnp.bfloat16), "dp"), axis=0
+    ).astype(jnp.float32)
     total_sq = lax.psum(jnp.sum(summed * summed), "mp")
     owned_grad = jnp.dot(my_slots, summed, precision=highest)
     clip_factor = jnp.minimum(1.0, math.sqrt(blocks * nseg * seg) / (jnp.sqrt(total_sq) + 1e-06))

time: 681 us -> 1440 us (2.11)
  waiting for transfers between devices: 587 us -> 1320 us
  other arithmetic: 13.5 us -> 33.5 us
    all_gather x0 -> x1, waiting for transfers between devices: none -> 956 us  [on_device(): lax.all_gather(local_grad.astype(jnp.float32).astype(jnp.bfloat16), 'dp')]
    psum x1 -> x0, waiting for transfers between devices: 218 us -> none  [on_device(): lax.psum(local_grad.astype(jnp.float32).astype(jnp.bfloat16), 'dp')]
    reduce_sum x0 -> x1, other arithmetic: none -> 20.1 us  [on_device(): jnp.sum(lax.all_gather(local_grad.astype(jnp.float32).astype(jnp.bfloat16...]
  transfers between devices with their start and end apart: 3 -> 3, of which waited for: 3 -> 3; matrix products, arithmetic and copies ran while one was open for 4% -> 2% of each run, Pallas kernels for 0% -> 0%
where the time goes in v1:
time: 1440 us
  waiting for transfers between devices  1320 us (92%)
  other arithmetic  33.5 us (2%)
  matrix products  32.3 us (2%)
  local copies, waits for them, and re-layouts  21.9 us (2%)
  between operations  14.8 us (1%)
    all_gather x1, waiting for transfers between devices, on_device(): lax.all_gather(local_grad.astype(jnp.float32).astype(jnp.bfloat16), 'dp')  956 us
    all_gather x1, waiting for transfers between devices, on_device(): lax.all_gather(new_master.astype(jnp.bfloat16), 'dp', axis=0, tiled=True)  361 us
  transfers between devices with their start and end apart: 3, of which 3 were waited for; matrix products, arithmetic and copies ran while one was open for 2% of the time, Pallas kernels for 0%

profile of v1, /device:TPU:0, one launch (start us, length us, event | category | flops | bytes accessed | tf_op | source)
XLA Modules:
  0.0 1439.4 jit_solution(7644665724312469854)
XLA Ops:
  7.2 0.0 copy-start.2
  7.2 0.0 all-gather.5.cloned.1.call-start
  7.2 0.7 all-gather.5.cloned.1.call-update
  7.9 0.0 copy-done.2
  7.9 0.2 convert_reduce_fusion
  8.2 956.4 %all-gather.5.cloned.1.call-done = bf16[8,1,192,16384]{3,2,1,0:T(8,128)(2,1)} async-done(((bf16[1,1,192,16384]{3,2,1,0:T(8,128)(2,1)}), bf16[8,1,192,16384]{3,2,1,0:T(8,128)(2,1)}) %all-gather.5.cloned.1.call-update) | async-done | bytes 50331664 | tf_op jit(solution)/shard_map/all_gather | solution.py:32
  964.6 20.1 %reduce_sum.50 = bf16[192,16384]{1,0:T(8,128)(2,1)} reduce(bf16[8,1,192,16384]{3,2,1,0:T(8,128)(2,1)} %all-gather.5.cloned.1.call-done, bf16[]{:T(256)} %constant.13.clone.1), dimensions={0,1}, to_apply=%region_2.0 | reduce | flops 22020096 | bytes 56623104 | tf_op jit(solution)/shard_map/reduce_sum | solution.py:31
  984.7 6.6 multiply_reduce_fusion
  991.3 0.1 convert_reduce_fusion.1
  991.4 7.7 psum.7
  999.8 0.0 copy-start
  999.8 14.0 convert_bitcast_fusion
  1013.8 0.0 copy-done
  1013.8 8.4 fusion.6
  1022.3 5.3 all-to-all-start
  1027.6 0.3 all-gather.7.cloned.1.call-start
  1027.9 0.5 all-gather.7.cloned.1.call-update
  1028.4 0.0 copy-start.1
  1028.4 5.7 copy.34
  1034.1 0.0 copy-done.1
  1034.1 3.8 copy.33
  1037.9 3.8 copy.32
  1041.8 360.6 %all-gather.7.cloned.1.call-done = bf16[8,36,16384]{2,1,0:T(8,128)(2,1)} async-done(((bf16[1,36,16384]{2,1,0:T(8,128)(2,1)}), bf16[8,36,16384]{2,1,0:T(8,128)(2,1)}) %all-gather.7.cloned.1.call-update) | async-done | bytes 9437200 | tf_op jit(solution)/shard_map/all_gather | solution.py:51
  1402.4 8.5 reshape.27
  1410.9 9.9 fusion
  1420.7 5.4 all-to-all-done
  1426.1 6.5 reduce_sum.52
  (2 shorter events, 0.1 us)
Async XLA Ops:
  7.2 0.8 copy-start.2
  7.2 957.4 %all-gather.5.cloned.1.call-start = ((), (), s32[]{:S(2)}) async-start(), calls=%async_computation.1 | async-start | bytes 56623104 | tf_op jit(solution)/shard_map/all_gather | solution.py:32
  999.8 14.0 copy-start
  1022.3 403.8 %all-to-all-start = ((f32[8,24,16384]{2,1,0:T(8,128)}), f32[8,24,16384]{2,1,0:T(8,128)}, u32[]{:S(2)}, u32[]{:S(2)}) async-start(f32[8,24,16384]{2,1,0:T(8,128)} %bitcast.44), calls=%async_computation | async-start | bytes 25165824 | tf_op jit(solution)/shard_map/all_to_all | solution.py:56
  1027.6 374.8 %all-gather.7.cloned.1.call-start = ((), (), s32[]{:S(2)}) async-start(), calls=%async_computation.2 | async-start | bytes 11796480 | tf_op jit(solution)/shard_map/all_gather | solution.py:51
  1028.4 5.7 copy-start.1
Sparse Core Ops, SparseCore 0:
  9.5 955.0 all-gather.4
  1031.2 371.1 all-gather.6
